TPU v7x, 32 devices: a whole 2x2x4 slice. The times are simulated.
32 devices in a mesh: member: 4 (over y, core), band: 8 (over z, x).
Axes of the slice: x: 2, y: 2, z: 4, core: 2. Of those that a mesh axis runs over, the one named last changes fastest.
Arguments:
- obs_values: bfloat16 [65536, 128], P(('member', 'band')), parts along dimension 0, may hold values from -6 to 6
- obs_band: int32 [65536, 1], P(('member', 'band')), parts along dimension 0, may hold values from 0 to 7; in each aligned block of 2048 rows (0 to 2047, 2048 to 4095, ...) at most 256 rows name the same one
- obs_cell: int32 [65536], P(('member', 'band')), parts along dimension 0, may hold values from 0 to 2047
- obs_offset: int32 [65536], P(('member', 'band')), parts along dimension 0, may hold values from 0 to 7
- sat_values: bfloat16 [65536, 128], P(('member', 'band')), parts along dimension 0, may hold values from -6 to 6
- sat_cell: int32 [65536], P(('member', 'band')), parts along dimension 0, may hold values from 0 to 2047
- sat_offset: int32 [65536], P(('member', 'band')), parts along dimension 0, may hold values from 0 to 7
- density_embed: float32 [128], replicated, may hold values from -3 to 3
- conv1_weight: bfloat16 [3, 3, 128, 128], replicated, may hold values from -0.1875 to 0.1875
- conv1_bias: float32 [128], replicated, may hold values from -3 to 3
- conv2_weight: bfloat16 [3, 3, 128, 256], replicated, may hold values from -0.1875 to 0.1875
- conv2_bias: float32 [256], replicated, may hold values from -3 to 3
- proj_weight: bfloat16 [256, 256], replicated, may hold values from -0.375 to 0.375
Outputs:
- latents: bfloat16 [64, 64, 256], P('member'), parts along dimension 0
There are 4 independent parts, one for each index of `member`. A program takes and returns all parts, laid end to end along the dimension named above; an argument that names none is the same for every part. Nothing has to cross between parts.
Inputs may be any that keep to these rules, and one draw needn't show every extreme that they name: `obs_band`: among the station rows of one device, at most 256 name the same band, and in every draw some band is named by exactly 256 rows of some device.
All inputs are finite; a program needn't handle non-finite values.
Results may differ from a plain program's by a relative error of at most 0.0061.
Values may be sent and summed in bfloat16 or wider, within the bound.
No kernel may reach another device: no remote copies, remote signals or barrier semaphores. Data moves between devices by JAX's collectives and lax.ppermute only.
A program may use at most 64 MiB of HBM per device.

v0:
```python
import jax
import jax.numpy as jnp
from jax import lax
from jax.sharding import PartitionSpec as P

LAT_DEV = 8
LON = 256


def passed_along(value, axis, by):
    length = lax.axis_size(axis)
    pairs = [(i, i + by) for i in range(length) if 0 <= i + by < length]
    return lax.ppermute(value, axis, pairs)


def weights_of(offsets):
    return jnp.exp(-offsets.astype(jnp.float32) ** 2 / 32.0).astype(jnp.bfloat16)


def deposit(values, cells, offsets, total_cells):
    weight = weights_of(offsets)
    block = min(512, total_cells)
    count = total_cells // block

    def one_block(start):
        ids = start + jnp.arange(block, dtype=jnp.int32)
        table = jnp.where(
            ids[:, None] == cells[None, :], weight[None, :], jnp.zeros((), jnp.bfloat16)
        )
        sums = jnp.dot(table, values, preferred_element_type=jnp.float32)
        density = jnp.sum(table, axis=1, dtype=jnp.float32)
        return (sums, density)

    starts = jnp.arange(count, dtype=jnp.int32) * block
    sums, density = lax.map(one_block, starts)
    return (sums.reshape(total_cells, values.shape[1]), density.reshape(total_cells))


def strided(padded, weight, bias):
    count, width, chans = padded.shape
    grid = jnp.pad(padded, ((0, 1), (1, 1), (0, 0)))
    parted = grid.reshape((count + 1) // 2, 2, (width + 2) // 2, 2, chans)
    rows = (count - 1) // 2
    cols = width // 2
    total = jnp.zeros((rows * cols, weight.shape[3]), jnp.float32)
    for first in range(3):
        for second in range(3):
            piece = parted[
                first // 2 : first // 2 + rows,
                first % 2,
                second // 2 : second // 2 + cols,
                second % 2,
                :,
            ]
            total = total + jnp.dot(
                piece.reshape(rows * cols, chans),
                weight[first, second],
                preferred_element_type=jnp.float32,
            )
    return jax.nn.gelu(total + bias, approximate=False).reshape(rows, cols, weight.shape[3])


def project(latent, proj_weight):
    flat = jnp.dot(
        latent.reshape(-1, latent.shape[2]), proj_weight, preferred_element_type=jnp.float32
    )
    return flat.astype(jnp.bfloat16).reshape(latent.shape)


def body(
    obs_values,
    obs_band,
    obs_cell,
    obs_offset,
    sat_values,
    sat_cell,
    sat_offset,
    density_embed,
    conv1_weight,
    conv1_bias,
    conv2_weight,
    conv2_bias,
    proj_weight,
):
    bands = lax.axis_size("band")
    position_index = lax.axis_index("band")
    obs_rows, d_in = obs_values.shape
    capacity = obs_rows // 8
    band_cells = LAT_DEV * LON
    target = obs_band[:, 0]
    choose = (target[:, None] == jnp.arange(bands, dtype=jnp.int32)[None, :]).astype(jnp.int32)
    rank = jnp.cumsum(choose, axis=0) - 1
    slot = jnp.sum(rank * choose, axis=1)
    position = target * capacity + slot
    send_values = jnp.zeros((bands * capacity, d_in), jnp.bfloat16).at[position].set(obs_values)
    send_cells = jnp.full((bands * capacity,), -1, jnp.int32).at[position].set(obs_cell)
    send_offsets = jnp.zeros((bands * capacity,), jnp.int32).at[position].set(obs_offset)
    got_values, got_cells, got_offsets = (
        lax.all_to_all(
            send_values.reshape(bands, capacity, d_in),
            "band",
            split_axis=0,
            concat_axis=0,
            tiled=True,
        ),
        lax.all_to_all(
            send_cells.reshape(bands, capacity), "band", split_axis=0, concat_axis=0, tiled=True
        ),
        lax.all_to_all(
            send_offsets.reshape(bands, capacity), "band", split_axis=0, concat_axis=0, tiled=True
        ),
    )
    sat_sums, sat_density = deposit(sat_values, sat_cell, sat_offset, band_cells)
    flat_values = got_values.reshape(bands * capacity, d_in)
    flat_cells = got_cells.reshape(bands * capacity)
    flat_offsets = got_offsets.reshape(bands * capacity)
    sta_sums, sta_density = deposit(flat_values, flat_cells, flat_offsets, band_cells)
    sums = sat_sums + sta_sums
    density = sat_density + sta_density
    grid0 = sums / jnp.maximum(density, 1.0)[:, None] + density[:, None] * density_embed[None, :]
    grid0 = grid0.astype(jnp.bfloat16).reshape(LAT_DEV, LON, d_in)
    above = passed_along(grid0[-3:], "band", 1)
    hidden1 = strided(jnp.concatenate([above, grid0], axis=0), conv1_weight, conv1_bias)
    keep_rows = (jnp.arange(hidden1.shape[0]) > 0) | (position_index > 0)
    hidden1 = jnp.where(keep_rows[:, None, None], hidden1, 0.0).astype(jnp.bfloat16)
    latent = strided(hidden1, conv2_weight, conv2_bias).astype(jnp.bfloat16)
    return project(lax.all_gather(latent, "band", axis=0, tiled=True), proj_weight)


def solution(mesh):
    placed = (
        P(("member", "band"), None),
        P(("member", "band"), None),
        P(("member", "band")),
        P(("member", "band")),
        P(("member", "band"), None),
        P(("member", "band")),
        P(("member", "band")),
        P(),
        P(),
        P(),
        P(),
        P(),
        P(),
    )
    return jax.shard_map(
        body, mesh=mesh, in_specs=placed, out_specs=P("member", None, None), check_vma=False
    )
```

profile of v0, /device:TPU:0, one launch (start us, length us, event | category | flops | bytes accessed | tf_op | source)
XLA Modules:
  0.0 124.4 jit_solution(5386460355857521245)
XLA Ops:
  0.0 0.7 fusion.69
  0.7 2.3 %reduce-window.6 = s32[8,16,128]{2,1,0:T(8,128)S(1)} reduce-window(s32[8,16,128]{2,1,0:T(8,128)S(1)} %fusion.69, s32[]{:T(128)} %constant.58.clone.1), window={size=1x1x128 pad=0_0x0_0x127_0}, to_apply=%region_3.4 | reduce-window | flops 2080768 | bytes 131076 | tf_op jit(solution)/shard_map/reduce-window
  3.6 0.7 fusion.49
  4.3 0.7 compare_select_fusion.12
  5.0 8.8 %scatter_custom_fusion = s32[2048]{0:T(1024)} fusion(s32[2048]{0:T(1024)S(1)} %bitcast.206, s32[2048]{0:T(1024)} %param.19, s32[]{:T(128)} %constant.63.clone.1), kind=kCustom, calls=%fused_computation.158 | custom fusion | bytes 8704 | tf_op jit(solution)/shard_map/scatter | solution.py:96
  13.8 7.3 %all-to-all-start = ((s32[8,1,256]{2,1,0:T(1,128)}), s32[8,1,256]{2,1,0:T(1,128)S(1)}, u32[]{:S(2)}, u32[]{:S(2)}) async-start(s32[8,1,256]{2,1,0:T(1,128)} %bitcast.11), calls=%async_computation | async-start | bytes 16384 | tf_op jit(solution)/shard_map/all_to_all | solution.py:106
  21.1 0.7 exponential_convert_fusion
  21.8 8.8 %scatter_custom_fusion.1 = s32[2048]{0:T(1024)} fusion(s32[2048]{0:T(1024)S(1)} %bitcast.207, s32[2048]{0:T(1024)} %param.20, s32[]{:T(128)} %constant.58.clone.1), kind=kCustom, calls=%fused_computation.156 | custom fusion | bytes 8704 | tf_op jit(solution)/shard_map/scatter | solution.py:97
  30.6 6.0 %all-to-all-start.1 = ((s32[8,1,256]{2,1,0:T(1,128)}), s32[8,1,256]{2,1,0:T(1,128)S(1)}, u32[]{:S(2)}, u32[]{:S(2)}) async-start(s32[8,1,256]{2,1,0:T(1,128)} %bitcast.12), calls=%async_computation.1 | async-start | bytes 16384 | tf_op jit(solution)/shard_map/all_to_all | solution.py:109
  36.6 6.8 %scatter_custom_fusion.2 = bf16[2048,128]{1,0:T(8,128)(2,1)} fusion(s32[2048]{0:T(1024)S(1)} %bitcast.208, bf16[2048,128]{1,0:T(8,128)(2,1)} %param.17, bf16[]{:T(256)} %constant.66.clone.1), kind=kCustom, calls=%fused_computation.77 | custom fusion | bytes 524800 | tf_op jit(solution)/shard_map/scatter | solution.py:95
  43.4 6.1 %all-to-all-start.2 = ((bf16[8,256,128]{2,1,0:T(8,128)(2,1)}), bf16[8,256,128]{2,1,0:T(8,128)(2,1)S(1)}, u32[]{:S(2)}, u32[]{:S(2)}) async-start(bf16[8,256,128]{2,1,0:T(8,128)(2,1)} %bitcast.13), calls=%async_computation.2 | async-start | bytes 1048576 | tf_op jit(solution)/shard_map/all_to_all | solution.py:99
  49.7 11.0 %while.24 = (s32[]{:T(128)}, f32[4,512,128]{2,1,0:T(8,128)S(1)}, f32[4,512]{1,0:T(4,128)S(1)}, s32[4]{0:T(128)S(1)}, s32[2048]{0:T(1024)S(1)}, /*index=5*/bf16[2...) while((s32[]{:T(128)}, f32[4,512,128]{2,1,0:T(8,128)S(1)}, ...), condition=%wide.region_2.3_spmd, body=%wide.region_0.2_spmd.sunk | while | flops 274726912 | bytes 823413 | solution.py:35
  50.3 0.7 iota_add_fusion.4
  51.0 0.8 fusion.128
  53.8 0.8 fusion.128
  55.8 0.7 iota_add_fusion.4
  56.5 0.8 fusion.128
  59.3 0.8 fusion.128
  60.7 2.2 %all-to-all-done.2 = bf16[8,256,128]{2,1,0:T(8,128)(2,1)S(1)} async-done(((bf16[8,256,128]{2,1,0:T(8,128)(2,1)}), bf16[8,256,128]{2,1,0:T(8,128)(2,1)S(1)}, u32[]{:S(2)}, u32[]{:S(2)}) %all-to-all-start.2) | async-done | bytes 524320 | tf_op jit(solution)/shard_map/all_to_all | solution.py:99
  63.0 10.6 %while.25 = (s32[]{:T(128)}, f32[4,512,128]{2,1,0:T(8,128)S(1)}, f32[4,512]{1,0:T(4,128)S(1)}, s32[4]{0:T(128)S(1)}, s32[8,256]{1,0:T(8,128)S(1)}, /*index=5*/bf...) while((s32[]{:T(128)}, f32[4,512,128]{2,1,0:T(8,128)S(1)}, ...), condition=%wide.region_11.12_spmd, body=%wide.region_9.11_spmd.sunk | while | flops 274726912 | bytes 839797 | solution.py:35
  64.3 0.8 fusion.130
  66.9 0.8 fusion.130
  69.5 0.8 fusion.130
  72.2 0.8 fusion.130
  74.6 3.6 %collective-permute-start = (bf16[3,256,128]{2,1,0:T(8,128)(2,1)S(1)}, bf16[3,256,128]{2,1,0:T(8,128)(2,1)S(1)}, u32[]{:S(2)}, u32[]{:S(2)}) collective-permute-start(bf16[3,256,128]{2,1,0:T(8,128)(2,1)S(1)} %bitcast.185), channel_id=1, source_target_pairs={{0,1},{1,2},{2,3},{3,4},{4,5},{5,6},{6,7},{8,9},{9,10},{10,11},{11... | collective-permute-start | bytes 589832 | tf_op jit(solution)/shard_map/ppermute | solution.py:13
  78.2 0.7 add_convert_fusion
  78.9 2.2 %collective-permute-done = bf16[3,256,128]{2,1,0:T(8,128)(2,1)S(1)} collective-permute-done((bf16[3,256,128]{2,1,0:T(8,128)(2,1)S(1)}, bf16[3,256,128]{2,1,0:T(8,128)(2,1)S(1)}, u32[]{:S(2)}, u32[]{:S(2)}) %collective-permute-start) | collective-permute-done | bytes 196640 | tf_op jit(solution)/shard_map/ppermute | solution.py:13
  81.6 3.2 %fusion.99 = (bf16[5,1,128,1,128]{4,3,2,1,0:T(2,128)(2,1)S(1)}, bf16[5,1,128,1,128]{4,3,2,1,0:T(2,128)(2,1)S(1)}, bf16[5,1,128,1,128]{4,3,2,1,0:T(2,128)(2,1)S(1...) fusion(bf16[6,2,129,2,128]{4,3,2,1,0:T(2,128)(2,1)S(1)} %reshap, ...), kind=kLoop, calls=%fused_computation.162 | loop fusion | bytes 2949120 | tf_op jit(solution)/shard_map/slice | solution.py:48
  85.1 0.8 copy-done.2
  87.7 0.9 fusion.28
  91.7 31.6 %all_gather.3 = bf16[16,64,256]{2,1,0:T(8,128)(2,1)S(1)} all-gather(bf16[2,64,256]{2,1,0:T(8,128)(2,1)S(1)} %bitcast.200), channel_id=1, replica_groups=mesh['member'=4,'band'=8] {'band'}, dimensions={0}, use_global_device_ids=true | all-gather | bytes 589824 | tf_op jit(solution)/shard_map/all_gather | solution.py:127
  123.3 1.1 convolution_convert_fusion
  (113 shorter events, 20.8 us)
Async XLA Ops:
  0.0 123.3 %copy-start = (bf16[256,256]{1,0:T(8,128)(2,1)S(1)}, bf16[256,256]{1,0:T(8,128)(2,1)}, u32[]{:S(2)}) copy-start(bf16[256,256]{1,0:T(8,128)(2,1)} %param.29) | copy-start | bytes 393220
  13.8 16.8 %all-to-all-start = ((s32[8,1,256]{2,1,0:T(1,128)}), s32[8,1,256]{2,1,0:T(1,128)S(1)}, u32[]{:S(2)}, u32[]{:S(2)}) async-start(s32[8,1,256]{2,1,0:T(1,128)} %bitcast.11), calls=%async_computation | async-start | bytes 16384 | tf_op jit(solution)/shard_map/all_to_all | solution.py:106
  30.6 12.9 %all-to-all-start.1 = ((s32[8,1,256]{2,1,0:T(1,128)}), s32[8,1,256]{2,1,0:T(1,128)S(1)}, u32[]{:S(2)}, u32[]{:S(2)}) async-start(s32[8,1,256]{2,1,0:T(1,128)} %bitcast.12), calls=%async_computation.1 | async-start | bytes 16384 | tf_op jit(solution)/shard_map/all_to_all | solution.py:109
  43.4 6.2 %copy-start.3 = (s32[2048]{0:T(1024)S(1)}, s32[2048]{0:T(1024)}, u32[]{:S(2)}) copy-start(s32[2048]{0:T(1024)} %param.22) | copy-start | bytes 24580
  43.4 6.2 %copy-start.5 = (bf16[2048,128]{1,0:T(8,128)(2,1)S(1)}, bf16[2048,128]{1,0:T(8,128)(2,1)}, u32[]{:S(2)}) copy-start(bf16[2048,128]{1,0:T(8,128)(2,1)} %param.21) | copy-start | bytes 1572868
  43.4 19.5 %all-to-all-start.2 = ((bf16[8,256,128]{2,1,0:T(8,128)(2,1)}), bf16[8,256,128]{2,1,0:T(8,128)(2,1)S(1)}, u32[]{:S(2)}, u32[]{:S(2)}) async-start(bf16[8,256,128]{2,1,0:T(8,128)(2,1)} %bitcast.13), calls=%async_computation.2 | async-start | bytes 1048576 | tf_op jit(solution)/shard_map/all_to_all | solution.py:99
  73.6 0.7 copy-start.4
  74.6 6.5 %collective-permute-start = (bf16[3,256,128]{2,1,0:T(8,128)(2,1)S(1)}, bf16[3,256,128]{2,1,0:T(8,128)(2,1)S(1)}, u32[]{:S(2)}, u32[]{:S(2)}) collective-permute-start(bf16[3,256,128]{2,1,0:T(8,128)(2,1)S(1)} %bitcast.185), channel_id=1, source_target_pairs={{0,1},{1,2},{2,3},{3,4},{4,5},{5,6},{6,7},{8,9},{9,10},{10,11},{11... | collective-permute-start | bytes 589832 | tf_op jit(solution)/shard_map/ppermute | solution.py:13
  85.0 1.0 copy-start.2
  87.1 0.7 copy-start.7
  89.0 1.1 copy-start.1
  90.3 0.9 copy-start.6
where the time goes:
time: 125 us; the launch traced here: 124 us
  local copies, waits for them, and re-layouts  36.9 us (30%)
  blocking collectives  31.6 us (25%)
  starting transfers between devices  23 us (18%)
  other arithmetic  16.6 us (13%)
  matrix products  11.1 us (9%)
  waiting for transfers between devices  4.46 us (4%)
    all_gather x1, blocking collectives, body(): lax.all_gather(latent, 'band', axis=0, tiled=True)  31.6 us
    scatter x1, local copies, waits for them, and re-layouts, body(): jnp.full((bands * capacity,), -1, jnp.int32).at[position].set(obs_cell)  8.78 us
    scatter x1, local copies, waits for them, and re-layouts, body(): jnp.zeros((bands * capacity,), jnp.int32).at[position].set(obs_offset)  8.78 us
    all_to_all x1, starting transfers between devices, body(): lax.all_to_all(send_cells.reshape(bands, capacity), 'band', split_axis=0,...  7.28 us
    scatter x1, local copies, waits for them, and re-layouts, body(): jnp.zeros((bands * capacity, d_in), jnp.bfloat16).at[position]  6.85 us
    all_to_all x1, starting transfers between devices, body(): lax.all_to_all(send_values.reshape(bands, capacity, d_in), 'band', split_...  6.12 us
    dot_general x8, matrix products, one_block(): sums = jnp.dot(table, values, preferred_element_type=jnp.float32)  6.09 us
    all_to_all x1, starting transfers between devices, body(): lax.all_to_all(send_offsets.reshape(bands, capacity), 'band', split_axis=...  6 us
  transfers between devices with their start and end apart: 4, of which 2 were waited for; matrix products, arithmetic and copies ran while one was open for 23% of the time, Pallas kernels for 0%

commit v1 on v0

--- a/solution.py
+++ b/solution.py
@@ -5,6 +5,27 @@
 
 LAT_DEV = 8
 LON = 256
+
+
+def joined_along(parts, dim):
+    parts = jnp.moveaxis(parts, 0, dim)
+    lengths = parts.shape
+    return parts.reshape(*lengths[:dim], lengths[dim] * lengths[dim + 1], *lengths[dim + 2 :])
+
+
+def collected_by_bits(x, axis):
+    length, index = (lax.axis_size(axis), lax.axis_index(axis))
+    parts, bit = (x[None], 1)
+    while bit < length:
+        other = lax.ppermute(parts, axis, [(i, i ^ bit) for i in range(length)])
+        low = index & bit == 0
+        parts = jnp.concatenate([jnp.where(low, parts, other), jnp.where(low, other, parts)])
+        bit *= 2
+    return parts
+
+
+def gather_by_bits(x, axis, dim):
+    return joined_along(collected_by_bits(x, axis), dim)
 
 
 def passed_along(value, axis, by):
@@ -124,7 +145,7 @@
     keep_rows = (jnp.arange(hidden1.shape[0]) > 0) | (position_index > 0)
     hidden1 = jnp.where(keep_rows[:, None, None], hidden1, 0.0).astype(jnp.bfloat16)
     latent = strided(hidden1, conv2_weight, conv2_bias).astype(jnp.bfloat16)
-    return project(lax.all_gather(latent, "band", axis=0, tiled=True), proj_weight)
+    return project(gather_by_bits(latent, "band", 0), proj_weight)
 
 
 def solution(mesh):

time: 125 us -> 116 us (0.928)
  blocking collectives: 31.6 us -> 0 us
  waiting for transfers between devices: 4.46 us -> 20.4 us
  starting transfers between devices: 23 us -> 29.5 us
    all_gather x1 -> x0, blocking collectives: 31.6 us -> none  [body(): lax.all_gather(latent, 'band', axis=0, tiled=True)]
    ppermute x0 -> x3, waiting for transfers between devices: none -> 15.5 us  [collected_by_bits(): other = lax.ppermute(parts, axis, [(i, i ^ bit) for i in range(length)])]
    ppermute x0 -> x3, starting transfers between devices: none -> 6.5 us  [collected_by_bits(): other = lax.ppermute(parts, axis, [(i, i ^ bit) for i in range(length)])]
  transfers between devices with their start and end apart: 4 -> 7, of which waited for: 2 -> 5; matrix products, arithmetic and copies ran while one was open for 23% -> 24% of each run, Pallas kernels for 0% -> 0%
where the time goes in v1:
time: 116 us; the launch traced here: 115 us
  local copies, waits for them, and re-layouts  36.7 us (32%)
  starting transfers between devices  29.5 us (25%)
  waiting for transfers between devices  20.4 us (18%)
  other arithmetic  16.5 us (14%)
  matrix products  11.1 us (10%)
    ppermute x3, waiting for transfers between devices, collected_by_bits(): other = lax.ppermute(parts, axis, [(i, i ^ bit) for i in range(length)])  15.5 us
    scatter x1, local copies, waits for them, and re-layouts, body(): jnp.full((bands * capacity,), -1, jnp.int32).at[position].set(obs_cell)  8.78 us
    scatter x1, local copies, waits for them, and re-layouts, body(): jnp.zeros((bands * capacity,), jnp.int32).at[position].set(obs_offset)  8.77 us
    all_to_all x1, starting transfers between devices, body(): lax.all_to_all(send_cells.reshape(bands, capacity), 'band', split_axis=0,...  7.28 us
    scatter x1, local copies, waits for them, and re-layouts, body(): jnp.zeros((bands * capacity, d_in), jnp.bfloat16).at[position]  6.85 us
    ppermute x3, starting transfers between devices, collected_by_bits(): other = lax.ppermute(parts, axis, [(i, i ^ bit) for i in range(length)])  6.5 us
    all_to_all x1, starting transfers between devices, body(): lax.all_to_all(send_values.reshape(bands, capacity, d_in), 'band', split_...  6.12 us
    dot_general x8, matrix products, one_block(): sums = jnp.dot(table, values, preferred_element_type=jnp.float32)  6.09 us
  transfers between devices with their start and end apart: 7, of which 5 were waited for; matrix products, arithmetic and copies ran while one was open for 24% of the time, Pallas kernels for 0%

profile of v1, /device:TPU:0, one launch (start us, length us, event | category | flops | bytes accessed | tf_op | source)
XLA Modules:
  0.0 115.0 jit_solution(15023025350626127335)
XLA Ops:
  0.0 0.7 fusion.69
  0.7 2.3 %reduce-window.6 = s32[8,16,128]{2,1,0:T(8,128)S(1)} reduce-window(s32[8,16,128]{2,1,0:T(8,128)S(1)} %fusion.69, s32[]{:T(128)} %constant.63.clone.1), window={size=1x1x128 pad=0_0x0_0x127_0}, to_apply=%region_3.4 | reduce-window | flops 2080768 | bytes 131076 | tf_op jit(solution)/shard_map/reduce-window
  3.6 0.7 fusion.49
  5.0 8.8 %scatter_custom_fusion = s32[2048]{0:T(1024)} fusion(s32[2048]{0:T(1024)S(1)} %bitcast.207, s32[2048]{0:T(1024)} %param.19, s32[]{:T(128)} %constant.69.clone.1), kind=kCustom, calls=%fused_computation.167 | custom fusion | bytes 8704 | tf_op jit(solution)/shard_map/scatter | solution.py:117
  13.8 7.3 %all-to-all-start = ((s32[8,1,256]{2,1,0:T(1,128)}), s32[8,1,256]{2,1,0:T(1,128)S(1)}, u32[]{:S(2)}, u32[]{:S(2)}) async-start(s32[8,1,256]{2,1,0:T(1,128)} %bitcast.11), calls=%async_computation | async-start | bytes 16384 | tf_op jit(solution)/shard_map/all_to_all | solution.py:127
  21.8 8.8 %scatter_custom_fusion.1 = s32[2048]{0:T(1024)} fusion(s32[2048]{0:T(1024)S(1)} %bitcast.208, s32[2048]{0:T(1024)} %param.20, s32[]{:T(128)} %constant.63.clone.1), kind=kCustom, calls=%fused_computation.165 | custom fusion | bytes 8704 | tf_op jit(solution)/shard_map/scatter | solution.py:118
  30.6 6.0 %all-to-all-start.1 = ((s32[8,1,256]{2,1,0:T(1,128)}), s32[8,1,256]{2,1,0:T(1,128)S(1)}, u32[]{:S(2)}, u32[]{:S(2)}) async-start(s32[8,1,256]{2,1,0:T(1,128)} %bitcast.12), calls=%async_computation.1 | async-start | bytes 16384 | tf_op jit(solution)/shard_map/all_to_all | solution.py:130
  36.6 6.8 %scatter_custom_fusion.2 = bf16[2048,128]{1,0:T(8,128)(2,1)} fusion(s32[2048]{0:T(1024)S(1)} %bitcast.209, bf16[2048,128]{1,0:T(8,128)(2,1)} %param.17, bf16[]{:T(256)} %constant.72.clone.1), kind=kCustom, calls=%fused_computation.79 | custom fusion | bytes 524800 | tf_op jit(solution)/shard_map/scatter | solution.py:116
  43.4 6.1 %all-to-all-start.2 = ((bf16[8,256,128]{2,1,0:T(8,128)(2,1)}), bf16[8,256,128]{2,1,0:T(8,128)(2,1)S(1)}, u32[]{:S(2)}, u32[]{:S(2)}) async-start(bf16[8,256,128]{2,1,0:T(8,128)(2,1)} %bitcast.13), calls=%async_computation.2 | async-start | bytes 1048576 | tf_op jit(solution)/shard_map/all_to_all | solution.py:120
  49.7 10.5 %while.24 = (s32[]{:T(128)}, f32[4,512,128]{2,1,0:T(8,128)S(1)}, f32[4,512]{1,0:T(4,128)S(1)}, s32[4]{0:T(128)S(1)}, s32[2048]{0:T(1024)S(1)}, /*index=5*/bf16[2...) while((s32[]{:T(128)}, f32[4,512,128]{2,1,0:T(8,128)S(1)}, ...), condition=%wide.region_2.3_spmd, body=%wide.region_0.2_spmd.sunk | while | flops 274726912 | bytes 823413 | solution.py:56
  50.9 0.8 fusion.128
  53.6 0.8 fusion.128
  56.2 0.8 fusion.128
  58.8 0.8 fusion.128
  60.3 2.7 %all-to-all-done.2 = bf16[8,256,128]{2,1,0:T(8,128)(2,1)S(1)} async-done(((bf16[8,256,128]{2,1,0:T(8,128)(2,1)}), bf16[8,256,128]{2,1,0:T(8,128)(2,1)S(1)}, u32[]{:S(2)}, u32[]{:S(2)}) %all-to-all-start.2) | async-done | bytes 524320 | tf_op jit(solution)/shard_map/all_to_all | solution.py:120
  63.0 10.6 %while.25 = (s32[]{:T(128)}, f32[4,512,128]{2,1,0:T(8,128)S(1)}, f32[4,512]{1,0:T(4,128)S(1)}, s32[4]{0:T(128)S(1)}, s32[8,256]{1,0:T(8,128)S(1)}, /*index=5*/bf...) while((s32[]{:T(128)}, f32[4,512,128]{2,1,0:T(8,128)S(1)}, ...), condition=%wide.region_11.12_spmd, body=%wide.region_9.11_spmd.sunk | while | flops 274726912 | bytes 839797 | solution.py:56
  64.3 0.8 fusion.130
  66.9 0.8 fusion.130
  69.5 0.8 fusion.130
  72.2 0.8 fusion.130
  74.6 3.6 %collective-permute-start = (bf16[3,256,128]{2,1,0:T(8,128)(2,1)S(1)}, bf16[3,256,128]{2,1,0:T(8,128)(2,1)S(1)}, u32[]{:S(2)}, u32[]{:S(2)}) collective-permute-start(bf16[3,256,128]{2,1,0:T(8,128)(2,1)S(1)} %bitcast.185), channel_id=1, source_target_pairs={{0,1},{1,2},{2,3},{3,4},{4,5},{5,6},{6,7},{8,9},{9,10},{10,11},{11... | collective-permute-start | bytes 589832 | tf_op jit(solution)/shard_map/ppermute | solution.py:34
  78.9 2.2 %collective-permute-done = bf16[3,256,128]{2,1,0:T(8,128)(2,1)S(1)} collective-permute-done((bf16[3,256,128]{2,1,0:T(8,128)(2,1)S(1)}, bf16[3,256,128]{2,1,0:T(8,128)(2,1)S(1)}, u32[]{:S(2)}, u32[]{:S(2)}) %collective-permute-start) | collective-permute-done | bytes 196640 | tf_op jit(solution)/shard_map/ppermute | solution.py:34
  81.6 3.2 %fusion.99 = (bf16[5,1,128,1,128]{4,3,2,1,0:T(2,128)(2,1)S(1)}, bf16[5,1,128,1,128]{4,3,2,1,0:T(2,128)(2,1)S(1)}, bf16[5,1,128,1,128]{4,3,2,1,0:T(2,128)(2,1)S(1...) fusion(bf16[6,2,129,2,128]{4,3,2,1,0:T(2,128)(2,1)S(1)} %reshap, ...), kind=kLoop, calls=%fused_computation.171 | loop fusion | bytes 2949120 | tf_op jit(solution)/shard_map/slice | solution.py:69
  85.1 0.8 copy-done.2
  87.7 0.9 fusion.28
  91.7 2.5 %collective-permute-start.1 = (bf16[1,2,64,256]{3,2,1,0:T(8,128)(2,1)S(1)}, bf16[1,2,64,256]{3,2,1,0:T(8,128)(2,1)S(1)}, u32[]{:S(2)}, u32[]{:S(2)}) collective-permute-start(bf16[1,2,64,256]{3,2,1,0:T(8,128)(2,1)S(1)} %bitcast.200), channel_id=1, source_target_pairs={{0,1},{1,0},{2,3},{3,2},{4,5},{5,4},{6,7},{7,6},{8,9},{9,8},{10,11... | collective-permute-start | bytes 196616 | tf_op jit(solution)/shard_map/ppermute | solution.py:20
  94.3 2.2 %collective-permute-done.1 = bf16[1,2,64,256]{3,2,1,0:T(8,128)(2,1)S(1)} collective-permute-done((bf16[1,2,64,256]{3,2,1,0:T(8,128)(2,1)S(1)}, bf16[1,2,64,256]{3,2,1,0:T(8,128)(2,1)S(1)}, u32[]{:S(2)}, u32[]{:S(2)}) %collective-permute-start.1) | collective-permute-done | bytes 65568 | tf_op jit(solution)/shard_map/ppermute | solution.py:20
  96.5 2.3 %collective-permute-start.2 = (bf16[2,2,64,256]{3,2,1,0:T(8,128)(2,1)S(1)}, bf16[2,2,64,256]{3,2,1,0:T(8,128)(2,1)S(1)}, u32[]{:S(2)}, u32[]{:S(2)}) collective-permute-start(bf16[2,2,64,256]{3,2,1,0:T(8,128)(2,1)S(1)} %pad_maximum_fusion.2), channel_id=1, source_target_pairs={{0,2},{1,3},{2,0},{3,1},{4,6},{5,7},{6,4},{7,5},{8,10},{9,11},{10,... | collective-permute-start | bytes 393224 | tf_op jit(solution)/shard_map/ppermute | solution.py:20
  98.8 4.8 %collective-permute-done.2 = bf16[2,2,64,256]{3,2,1,0:T(8,128)(2,1)S(1)} collective-permute-done((bf16[2,2,64,256]{3,2,1,0:T(8,128)(2,1)S(1)}, bf16[2,2,64,256]{3,2,1,0:T(8,128)(2,1)S(1)}, u32[]{:S(2)}, u32[]{:S(2)}) %collective-permute-start.2) | collective-permute-done | bytes 131104 | tf_op jit(solution)/shard_map/ppermute | solution.py:20
  103.7 1.7 %collective-permute-start.3 = (bf16[4,2,64,256]{3,2,1,0:T(8,128)(2,1)S(1)}, bf16[4,2,64,256]{3,2,1,0:T(8,128)(2,1)S(1)}, u32[]{:S(2)}, u32[]{:S(2)}) collective-permute-start(bf16[4,2,64,256]{3,2,1,0:T(8,128)(2,1)S(1)} %pad_maximum_fusion.1), channel_id=1, source_target_pairs={{0,4},{1,5},{2,6},{3,7},{4,0},{5,1},{6,2},{7,3},{8,12},{9,13},{10,... | collective-permute-start | bytes 786440 | tf_op jit(solution)/shard_map/ppermute | solution.py:20
  105.4 8.5 %collective-permute-done.3 = bf16[4,2,64,256]{3,2,1,0:T(8,128)(2,1)S(1)} collective-permute-done((bf16[4,2,64,256]{3,2,1,0:T(8,128)(2,1)S(1)}, bf16[4,2,64,256]{3,2,1,0:T(8,128)(2,1)S(1)}, u32[]{:S(2)}, u32[]{:S(2)}) %collective-permute-start.3) | collective-permute-done | bytes 262176 | tf_op jit(solution)/shard_map/ppermute | solution.py:20
  113.9 1.1 convolution_convert_fusion
  (124 shorter events, 24.1 us)
Async XLA Ops:
  0.0 113.9 %copy-start = (bf16[256,256]{1,0:T(8,128)(2,1)S(1)}, bf16[256,256]{1,0:T(8,128)(2,1)}, u32[]{:S(2)}) copy-start(bf16[256,256]{1,0:T(8,128)(2,1)} %param.29) | copy-start | bytes 393220
  13.8 16.8 %all-to-all-start = ((s32[8,1,256]{2,1,0:T(1,128)}), s32[8,1,256]{2,1,0:T(1,128)S(1)}, u32[]{:S(2)}, u32[]{:S(2)}) async-start(s32[8,1,256]{2,1,0:T(1,128)} %bitcast.11), calls=%async_computation | async-start | bytes 16384 | tf_op jit(solution)/shard_map/all_to_all | solution.py:127
  30.6 12.9 %all-to-all-start.1 = ((s32[8,1,256]{2,1,0:T(1,128)}), s32[8,1,256]{2,1,0:T(1,128)S(1)}, u32[]{:S(2)}, u32[]{:S(2)}) async-start(s32[8,1,256]{2,1,0:T(1,128)} %bitcast.12), calls=%async_computation.1 | async-start | bytes 16384 | tf_op jit(solution)/shard_map/all_to_all | solution.py:130
  43.4 6.2 %copy-start.3 = (s32[2048]{0:T(1024)S(1)}, s32[2048]{0:T(1024)}, u32[]{:S(2)}) copy-start(s32[2048]{0:T(1024)} %param.22) | copy-start | bytes 24580
  43.4 6.2 %copy-start.5 = (bf16[2048,128]{1,0:T(8,128)(2,1)S(1)}, bf16[2048,128]{1,0:T(8,128)(2,1)}, u32[]{:S(2)}) copy-start(bf16[2048,128]{1,0:T(8,128)(2,1)} %param.21) | copy-start | bytes 1572868
  43.4 19.5 %all-to-all-start.2 = ((bf16[8,256,128]{2,1,0:T(8,128)(2,1)}), bf16[8,256,128]{2,1,0:T(8,128)(2,1)S(1)}, u32[]{:S(2)}, u32[]{:S(2)}) async-start(bf16[8,256,128]{2,1,0:T(8,128)(2,1)} %bitcast.13), calls=%async_computation.2 | async-start | bytes 1048576 | tf_op jit(solution)/shard_map/all_to_all | solution.py:120
  73.6 0.7 copy-start.4
  74.6 6.5 %collective-permute-start = (bf16[3,256,128]{2,1,0:T(8,128)(2,1)S(1)}, bf16[3,256,128]{2,1,0:T(8,128)(2,1)S(1)}, u32[]{:S(2)}, u32[]{:S(2)}) collective-permute-start(bf16[3,256,128]{2,1,0:T(8,128)(2,1)S(1)} %bitcast.185), channel_id=1, source_target_pairs={{0,1},{1,2},{2,3},{3,4},{4,5},{5,6},{6,7},{8,9},{9,10},{10,11},{11... | collective-permute-start | bytes 589832 | tf_op jit(solution)/shard_map/ppermute | solution.py:34
  85.0 1.0 copy-start.2
  87.1 0.7 copy-start.7
  89.0 1.1 copy-start.1
  90.3 0.9 copy-start.6
  91.7 4.8 %collective-permute-start.1 = (bf16[1,2,64,256]{3,2,1,0:T(8,128)(2,1)S(1)}, bf16[1,2,64,256]{3,2,1,0:T(8,128)(2,1)S(1)}, u32[]{:S(2)}, u32[]{:S(2)}) collective-permute-start(bf16[1,2,64,256]{3,2,1,0:T(8,128)(2,1)S(1)} %bitcast.200), channel_id=1, source_target_pairs={{0,1},{1,0},{2,3},{3,2},{4,5},{5,4},{6,7},{7,6},{8,9},{9,8},{10,11... | collective-permute-start | bytes 196616 | tf_op jit(solution)/shard_map/ppermute | solution.py:20
  96.5 7.1 %collective-permute-start.2 = (bf16[2,2,64,256]{3,2,1,0:T(8,128)(2,1)S(1)}, bf16[2,2,64,256]{3,2,1,0:T(8,128)(2,1)S(1)}, u32[]{:S(2)}, u32[]{:S(2)}) collective-permute-start(bf16[2,2,64,256]{3,2,1,0:T(8,128)(2,1)S(1)} %pad_maximum_fusion.2), channel_id=1, source_target_pairs={{0,2},{1,3},{2,0},{3,1},{4,6},{5,7},{6,4},{7,5},{8,10},{9,11},{10,... | collective-permute-start | bytes 393224 | tf_op jit(solution)/shard_map/ppermute | solution.py:20
  103.7 10.1 %collective-permute-start.3 = (bf16[4,2,64,256]{3,2,1,0:T(8,128)(2,1)S(1)}, bf16[4,2,64,256]{3,2,1,0:T(8,128)(2,1)S(1)}, u32[]{:S(2)}, u32[]{:S(2)}) collective-permute-start(bf16[4,2,64,256]{3,2,1,0:T(8,128)(2,1)S(1)} %pad_maximum_fusion.1), channel_id=1, source_target_pairs={{0,4},{1,5},{2,6},{3,7},{4,0},{5,1},{6,2},{7,3},{8,12},{9,13},{10,... | collective-permute-start | bytes 786440 | tf_op jit(solution)/shard_map/ppermute | solution.py:20
